TPU v7x, 256 devices: a whole 4x4x8 slice. The times are simulated.
256 devices in a mesh: dom: 16 (over z, core), grp: 16 (over y, x).
Axes of the slice: x: 4, y: 4, z: 8, core: 2. Of those that a mesh axis runs over, the one named last changes fastest.
Arguments:
- positions: float32 [65536, 3, 128], P(('dom', 'grp')), may hold values from -4 to 4
- velocities: float32 [65536, 3, 128], P(('dom', 'grp')), may hold values from -9 to 9
- masses: float32 [65536, 128], P(('dom', 'grp')), may hold values from 0.3 to 3
- destination: int32 [65536], P(('dom', 'grp')), may hold values from 0 to 15, as said below
- group_ids: int32 [65536, 128], P(('dom', 'grp')), may hold values from 0 to 1023, as said below
- boundary_set: int32 [256, 64], P(('dom', 'grp')), may hold values from 0 to 511, as said below
- send_list: int32 [256, 16, 16], P(('dom', 'grp')), may hold values from 0 to 63, as said below
- send_count: int32 [256, 16], P(('dom', 'grp')), may hold values from 0 to 16, as said below
- partners: int32 [131072, 4], P(('dom', 'grp')), may hold values from 0 to 767, as said below
Outputs:
- energy: float32 [65536, 128], P(('dom', 'grp'))
- group_kinetic: float32 [1024], replicated
Inputs may be any that keep to these rules, and one draw needn't show every extreme that they name: Each block of 256 leaves sends at most 32 leaves to one destination; in each dom index one destination receives exactly 32 leaves from every block. `group_ids`: the particles of block b carry the 16 group numbers 4 * b to 4 * b + 15, taken modulo 1024, each at least once and no others. `boundary_set`: each row holds 64 distinct slot numbers. `send_list`: each row of 16 holds distinct positions. `send_count`: A block sends nothing to its own grp index; in each dom index one grp index receives 16 from every other block. `partners`: each row holds 4 distinct entry numbers of combined.
All inputs are finite; a program needn't handle non-finite values.
Results may differ from a plain program's by a relative error of at most 0.0003.
Values sent between devices are 32-bit elements; how exact they have to be, the bound alone decides.
No kernel may reach another device: no remote copies, remote signals or barrier semaphores. Data moves between devices by JAX's collectives and lax.ppermute only.
A program may use at most 64 MiB of HBM per device.

v0:
```python
import jax
import jax.numpy as jnp
from jax import lax
from jax.sharding import PartitionSpec as P

GSPAN = 16
GROUP_DEV = 4
softening = 0.0025
exact = lax.Precision.HIGHEST


def select_rows(table, index):
    count = table.shape[0]
    flat = table.reshape(count, -1)
    picker = (index.reshape(-1)[:, None] == jnp.arange(count, dtype=jnp.int32)[None, :]).astype(
        jnp.float32
    )
    chosen = jnp.dot(picker, flat, precision=exact, preferred_element_type=jnp.float32)
    return chosen.reshape(index.shape + table.shape[1:])


def tile_potential(targets, sources):
    distance = softening
    for component in range(3):
        offset = targets[:, None, component, :, None] - sources[:, :, component, None, :]
        distance = distance + offset * offset
    weights = sources[:, :, 3, None, :] * lax.rsqrt(distance)
    return -jnp.sum(weights, axis=(1, 3))


def slot_potential(owned, combined, pair_index, coupling):
    slot_count = owned.shape[0]
    leaf_width = owned.shape[2]
    block_rows = max(32, slot_count // 16)

    def one_block(inputs):
        targets, indices = inputs
        sources = select_rows(combined, indices)
        return tile_potential(targets, sources)

    result = lax.map(
        one_block,
        (
            owned.reshape(slot_count // block_rows, block_rows, 4, leaf_width),
            pair_index.reshape(slot_count // block_rows, block_rows, pair_index.shape[1]),
        ),
    )
    return result.reshape(slot_count, leaf_width) * coupling


def shards(
    positions,
    velocities,
    masses,
    destination,
    group_ids,
    boundary_set,
    send_list,
    send_count,
    partners,
):
    owners = lax.axis_size("grp")
    leaves = positions.shape[0]
    leaf_width = positions.shape[2]
    capacity = 2 * leaves // owners
    slot_count = owners * capacity
    groups = GROUP_DEV * lax.axis_size("dom") * owners
    block_index = lax.axis_index("dom") * owners + lax.axis_index("grp")
    first_group = block_index * GROUP_DEV
    mass_flat = masses.reshape(-1)
    group_flat = group_ids.reshape(-1)
    speeds = jnp.transpose(velocities, (1, 0, 2)).reshape(3, -1)
    local_ids = (group_flat - first_group) % groups
    member = (jnp.arange(GSPAN, dtype=jnp.int32)[:, None] == local_ids[None, :]).astype(jnp.float32)
    place = (
        (first_group + jnp.arange(GSPAN, dtype=jnp.int32))[:, None] % groups
        == jnp.arange(groups, dtype=jnp.int32)[None, :]
    ).astype(jnp.float32)

    def group_sums(stats):
        local_sums = jnp.einsum(
            "kp,gp->kg", stats, member, precision=exact, preferred_element_type=jnp.float32
        )
        return jnp.dot(local_sums, place, precision=exact, preferred_element_type=jnp.float32)

    first_sums = group_sums(
        jnp.concatenate([mass_flat[None, :], mass_flat[None, :] * speeds], axis=0)
    )
    mass_total, momentum = lax.psum((first_sums[0], first_sums[1:]), ("dom", "grp"))
    bulk_velocity = momentum / mass_total[None, :]
    bulk_local = jnp.einsum(
        "kq,gq->kg", bulk_velocity, place, precision=exact, preferred_element_type=jnp.float32
    )
    per_particle = jnp.dot(bulk_local, member, precision=exact, preferred_element_type=jnp.float32)
    relative = speeds - per_particle
    kinetic = 0.5 * jnp.sum(relative * relative, axis=0)
    heat_sum = lax.psum(group_sums((mass_flat * kinetic)[None, :])[0], ("dom", "grp"))
    group_kinetic = heat_sum / mass_total
    onehot = (destination[:, None] == jnp.arange(owners, dtype=jnp.int32)[None, :]).astype(
        jnp.int32
    )
    leaf_rank = jnp.sum((jnp.cumsum(onehot, axis=0) - onehot) * onehot, axis=1)
    target = destination * capacity + leaf_rank
    payload = jnp.concatenate([positions, masses[:, None, :]], axis=1)
    placing = (jnp.arange(slot_count, dtype=jnp.int32)[:, None] == target[None, :]).astype(
        jnp.float32
    )
    outgoing = jnp.dot(
        placing, payload.reshape(leaves, -1), precision=exact, preferred_element_type=jnp.float32
    ).reshape(slot_count, 4, leaf_width)
    owned = lax.all_to_all(outgoing, "grp", split_axis=0, concat_axis=0, tiled=True)
    set_size = boundary_set.shape[1]
    per_peer = send_list.shape[2]
    boundary = select_rows(owned, boundary_set[0])
    every_set = lax.all_gather(boundary, "grp", axis=0, tiled=True)
    all_lists, all_counts = (
        lax.all_gather(send_list, "grp", axis=0, tiled=True),
        lax.all_gather(send_count, "grp", axis=0, tiled=True),
    )
    my_index = lax.axis_index("grp")
    my_lists = jnp.take(all_lists, my_index, axis=1)
    my_counts = jnp.take(all_counts, my_index, axis=1)
    positions_in = jnp.arange(owners, dtype=jnp.int32)[:, None] * set_size + my_lists
    remote = select_rows(every_set, positions_in)
    is_live = jnp.arange(per_peer, dtype=jnp.int32)[None, :] < my_counts[:, None]
    remote = jnp.where(is_live[:, :, None, None], remote, jnp.zeros_like(remote))
    remote = remote.reshape(owners * per_peer, 4, leaf_width)
    combined = jnp.concatenate([owned, remote], axis=0)
    coupling = 1.0 / (partners.shape[1] * leaf_width)
    potential = slot_potential(owned, combined, partners, coupling)
    returned = lax.all_to_all(potential, "grp", split_axis=0, concat_axis=0, tiled=True)
    own_potential = jnp.einsum(
        "sl,sp->lp", placing, returned, precision=exact, preferred_element_type=jnp.float32
    )
    energy = kinetic.reshape(leaves, leaf_width) + own_potential
    return (energy, group_kinetic)


def solution(mesh):
    in_specs = (
        P(("dom", "grp"), None, None),
        P(("dom", "grp"), None, None),
        P(("dom", "grp"), None),
        P(("dom", "grp")),
        P(("dom", "grp"), None),
        P(("dom", "grp"), None),
        P(("dom", "grp"), None, None),
        P(("dom", "grp"), None),
        P(("dom", "grp"), None),
    )
    out_specs = (P(("dom", "grp"), None), P())
    return jax.shard_map(shards, mesh=mesh, in_specs=in_specs, out_specs=out_specs, check_vma=False)
```

profile of v0, /device:TPU:1, one launch (start us, length us, event | category | flops | bytes accessed | tf_op | source)
XLA Modules:
  0.0 366.0 jit_solution(14305169449429546651)
XLA Ops:
  10.2 1.2 copy.63
  13.7 23.4 %all_to_all.14 = f32[512,4,128]{2,1,0:T(4,128)S(1)} all-to-all(f32[512,4,128]{2,1,0:T(4,128)S(1)} %copy.64), channel_id=1, replica_groups=mesh['dom'=16,'grp'=16] {'grp'}, dimensions={0} | all-to-all | bytes 2097152 | tf_op jit(solution)/shard_map/all_to_all | solution.py:111
  37.5 1.4 fusion.15
  39.4 1.6 fusion.9
  42.0 14.1 %all-gather = s32[16,1,16]{2,1,0:T(1,128)S(1)} all-gather(s32[1,1,16]{2,1,0:T(1,128)S(1)} %bitcast.158), channel_id=1, replica_groups=mesh['dom'=16,'grp'=16] {'grp'}, dimensions={0}, use_global_device_ids=true | all-gather | bytes 1088 | tf_op jit(solution)/shard_map/all_gather | solution.py:118
  56.6 17.3 %all_gather.10 = s32[16,16,16]{2,1,0:T(8,128)S(1)} all-gather(s32[1,16,16]{2,1,0:T(8,128)S(1)} %copy-done.7), channel_id=1, replica_groups=mesh['dom'=16,'grp'=16] {'grp'}, dimensions={0}, use_global_device_ids=true | all-gather | bytes 17408 | tf_op jit(solution)/shard_map/all_gather | solution.py:117
  73.9 89.0 %all-reduce = (f32[3,1024]{1,0:T(4,128)S(1)}, f32[1024]{0:T(1024)S(1)}) all-reduce(f32[3,1024]{1,0:T(4,128)S(1)} %slice.60, f32[1024]{0:T(1024)S(1)} %bitcast.154), channel_id=1, replica_groups=mesh['dom'=16,'grp'=16] {'dom','grp'}, use_global_device_ids=true, to_apply=%region_0.1 | all-reduce | flops 4096 | bytes 32768 | tf_op jit(solution)/shard_map/psum | solution.py:89
  165.0 1.9 copy.66
  166.9 1.3 fusion.10
  168.6 1.5 pad_maximum_fusion
  170.1 1.7 copy.70
  171.8 104.0 %while.12 = (s32[]{:T(128)}, f32[16,32,128]{2,1,0:T(8,128)S(1)}, s32[16,32,4]{1,0,2:T(8,128)}, f32[768,4,128]{0,2,1:T(8,128)S(1)}, f32[16,32,4,128]{3,2,1,0:T(4,128)S(1)}, /*index=5*/s32[]{:T(128)}) while((s32[]{:T(128)}, f32[16,32,128]{2,1,0:T(8,128)S(1)}, s32[16,32,4]{1,0,2:T(8,128)}, f32[768,4,128]{0,2,1:T(8,128)S(1)}, ...), condition=%wide.region_8.9_spmd, body=%wide.region_6.8_spmd.sunk | while | flops 627146752 | bytes 3606097 | solution.py:41
  174.0 4.4 %multiply_reduce_fusion.2 = f32[32,128]{1,0:T(8,128)S(1)} fusion(f32[32,4,128]{2,1,0:T(4,128)S(1)} %copy.88, f32[32,128]{1,0:T(8,128)S(1)} %get-tuple-element.135, f32[32,4,128]{2,1,0:T(4,128)S(1)} %copy.90, f32[32,128]{1,0:T(8,128)S(1)} %get-tuple-element.137, f32[32,4,128]{2,1,0:T(4,128)S(1)} %copy.91, f32[32,128]{1,0:T(8,128)S(1)} %get-tuple-element.139, ...), kind=kLoop, calls=%fused_computation.clone.1 | loop fusion | flops 23064576 | bytes 327680 | tf_op jit(solution)/shard_map/while/body/eval_jaxpr/reduce_sum | solution.py:28
  180.5 4.4 %multiply_reduce_fusion.2 = f32[32,128]{1,0:T(8,128)S(1)} fusion(f32[32,4,128]{2,1,0:T(4,128)S(1)} %copy.88, f32[32,128]{1,0:T(8,128)S(1)} %get-tuple-element.135, f32[32,4,128]{2,1,0:T(4,128)S(1)} %copy.90, f32[32,128]{1,0:T(8,128)S(1)} %get-tuple-element.137, f32[32,4,128]{2,1,0:T(4,128)S(1)} %copy.91, f32[32,128]{1,0:T(8,128)S(1)} %get-tuple-element.139, ...), kind=kLoop, calls=%fused_computation.clone.1 | loop fusion | flops 23064576 | bytes 327680 | tf_op jit(solution)/shard_map/while/body/eval_jaxpr/reduce_sum | solution.py:28
  187.0 4.4 %multiply_reduce_fusion.2 = f32[32,128]{1,0:T(8,128)S(1)} fusion(f32[32,4,128]{2,1,0:T(4,128)S(1)} %copy.88, f32[32,128]{1,0:T(8,128)S(1)} %get-tuple-element.135, f32[32,4,128]{2,1,0:T(4,128)S(1)} %copy.90, f32[32,128]{1,0:T(8,128)S(1)} %get-tuple-element.137, f32[32,4,128]{2,1,0:T(4,128)S(1)} %copy.91, f32[32,128]{1,0:T(8,128)S(1)} %get-tuple-element.139, ...), kind=kLoop, calls=%fused_computation.clone.1 | loop fusion | flops 23064576 | bytes 327680 | tf_op jit(solution)/shard_map/while/body/eval_jaxpr/reduce_sum | solution.py:28
  193.5 4.4 %multiply_reduce_fusion.2 = f32[32,128]{1,0:T(8,128)S(1)} fusion(f32[32,4,128]{2,1,0:T(4,128)S(1)} %copy.88, f32[32,128]{1,0:T(8,128)S(1)} %get-tuple-element.135, f32[32,4,128]{2,1,0:T(4,128)S(1)} %copy.90, f32[32,128]{1,0:T(8,128)S(1)} %get-tuple-element.137, f32[32,4,128]{2,1,0:T(4,128)S(1)} %copy.91, f32[32,128]{1,0:T(8,128)S(1)} %get-tuple-element.139, ...), kind=kLoop, calls=%fused_computation.clone.1 | loop fusion | flops 23064576 | bytes 327680 | tf_op jit(solution)/shard_map/while/body/eval_jaxpr/reduce_sum | solution.py:28
  200.0 4.4 %multiply_reduce_fusion.2 = f32[32,128]{1,0:T(8,128)S(1)} fusion(f32[32,4,128]{2,1,0:T(4,128)S(1)} %copy.88, f32[32,128]{1,0:T(8,128)S(1)} %get-tuple-element.135, f32[32,4,128]{2,1,0:T(4,128)S(1)} %copy.90, f32[32,128]{1,0:T(8,128)S(1)} %get-tuple-element.137, f32[32,4,128]{2,1,0:T(4,128)S(1)} %copy.91, f32[32,128]{1,0:T(8,128)S(1)} %get-tuple-element.139, ...), kind=kLoop, calls=%fused_computation.clone.1 | loop fusion | flops 23064576 | bytes 327680 | tf_op jit(solution)/shard_map/while/body/eval_jaxpr/reduce_sum | solution.py:28
  206.5 4.4 %multiply_reduce_fusion.2 = f32[32,128]{1,0:T(8,128)S(1)} fusion(f32[32,4,128]{2,1,0:T(4,128)S(1)} %copy.88, f32[32,128]{1,0:T(8,128)S(1)} %get-tuple-element.135, f32[32,4,128]{2,1,0:T(4,128)S(1)} %copy.90, f32[32,128]{1,0:T(8,128)S(1)} %get-tuple-element.137, f32[32,4,128]{2,1,0:T(4,128)S(1)} %copy.91, f32[32,128]{1,0:T(8,128)S(1)} %get-tuple-element.139, ...), kind=kLoop, calls=%fused_computation.clone.1 | loop fusion | flops 23064576 | bytes 327680 | tf_op jit(solution)/shard_map/while/body/eval_jaxpr/reduce_sum | solution.py:28
  213.0 4.4 %multiply_reduce_fusion.2 = f32[32,128]{1,0:T(8,128)S(1)} fusion(f32[32,4,128]{2,1,0:T(4,128)S(1)} %copy.88, f32[32,128]{1,0:T(8,128)S(1)} %get-tuple-element.135, f32[32,4,128]{2,1,0:T(4,128)S(1)} %copy.90, f32[32,128]{1,0:T(8,128)S(1)} %get-tuple-element.137, f32[32,4,128]{2,1,0:T(4,128)S(1)} %copy.91, f32[32,128]{1,0:T(8,128)S(1)} %get-tuple-element.139, ...), kind=kLoop, calls=%fused_computation.clone.1 | loop fusion | flops 23064576 | bytes 327680 | tf_op jit(solution)/shard_map/while/body/eval_jaxpr/reduce_sum | solution.py:28
  219.4 4.4 %multiply_reduce_fusion.2 = f32[32,128]{1,0:T(8,128)S(1)} fusion(f32[32,4,128]{2,1,0:T(4,128)S(1)} %copy.88, f32[32,128]{1,0:T(8,128)S(1)} %get-tuple-element.135, f32[32,4,128]{2,1,0:T(4,128)S(1)} %copy.90, f32[32,128]{1,0:T(8,128)S(1)} %get-tuple-element.137, f32[32,4,128]{2,1,0:T(4,128)S(1)} %copy.91, f32[32,128]{1,0:T(8,128)S(1)} %get-tuple-element.139, ...), kind=kLoop, calls=%fused_computation.clone.1 | loop fusion | flops 23064576 | bytes 327680 | tf_op jit(solution)/shard_map/while/body/eval_jaxpr/reduce_sum | solution.py:28
  225.9 4.4 %multiply_reduce_fusion.2 = f32[32,128]{1,0:T(8,128)S(1)} fusion(f32[32,4,128]{2,1,0:T(4,128)S(1)} %copy.88, f32[32,128]{1,0:T(8,128)S(1)} %get-tuple-element.135, f32[32,4,128]{2,1,0:T(4,128)S(1)} %copy.90, f32[32,128]{1,0:T(8,128)S(1)} %get-tuple-element.137, f32[32,4,128]{2,1,0:T(4,128)S(1)} %copy.91, f32[32,128]{1,0:T(8,128)S(1)} %get-tuple-element.139, ...), kind=kLoop, calls=%fused_computation.clone.1 | loop fusion | flops 23064576 | bytes 327680 | tf_op jit(solution)/shard_map/while/body/eval_jaxpr/reduce_sum | solution.py:28
  232.4 4.4 %multiply_reduce_fusion.2 = f32[32,128]{1,0:T(8,128)S(1)} fusion(f32[32,4,128]{2,1,0:T(4,128)S(1)} %copy.88, f32[32,128]{1,0:T(8,128)S(1)} %get-tuple-element.135, f32[32,4,128]{2,1,0:T(4,128)S(1)} %copy.90, f32[32,128]{1,0:T(8,128)S(1)} %get-tuple-element.137, f32[32,4,128]{2,1,0:T(4,128)S(1)} %copy.91, f32[32,128]{1,0:T(8,128)S(1)} %get-tuple-element.139, ...), kind=kLoop, calls=%fused_computation.clone.1 | loop fusion | flops 23064576 | bytes 327680 | tf_op jit(solution)/shard_map/while/body/eval_jaxpr/reduce_sum | solution.py:28
  238.9 4.4 %multiply_reduce_fusion.2 = f32[32,128]{1,0:T(8,128)S(1)} fusion(f32[32,4,128]{2,1,0:T(4,128)S(1)} %copy.88, f32[32,128]{1,0:T(8,128)S(1)} %get-tuple-element.135, f32[32,4,128]{2,1,0:T(4,128)S(1)} %copy.90, f32[32,128]{1,0:T(8,128)S(1)} %get-tuple-element.137, f32[32,4,128]{2,1,0:T(4,128)S(1)} %copy.91, f32[32,128]{1,0:T(8,128)S(1)} %get-tuple-element.139, ...), kind=kLoop, calls=%fused_computation.clone.1 | loop fusion | flops 23064576 | bytes 327680 | tf_op jit(solution)/shard_map/while/body/eval_jaxpr/reduce_sum | solution.py:28
  245.4 4.4 %multiply_reduce_fusion.2 = f32[32,128]{1,0:T(8,128)S(1)} fusion(f32[32,4,128]{2,1,0:T(4,128)S(1)} %copy.88, f32[32,128]{1,0:T(8,128)S(1)} %get-tuple-element.135, f32[32,4,128]{2,1,0:T(4,128)S(1)} %copy.90, f32[32,128]{1,0:T(8,128)S(1)} %get-tuple-element.137, f32[32,4,128]{2,1,0:T(4,128)S(1)} %copy.91, f32[32,128]{1,0:T(8,128)S(1)} %get-tuple-element.139, ...), kind=kLoop, calls=%fused_computation.clone.1 | loop fusion | flops 23064576 | bytes 327680 | tf_op jit(solution)/shard_map/while/body/eval_jaxpr/reduce_sum | solution.py:28
  251.9 4.4 %multiply_reduce_fusion.2 = f32[32,128]{1,0:T(8,128)S(1)} fusion(f32[32,4,128]{2,1,0:T(4,128)S(1)} %copy.88, f32[32,128]{1,0:T(8,128)S(1)} %get-tuple-element.135, f32[32,4,128]{2,1,0:T(4,128)S(1)} %copy.90, f32[32,128]{1,0:T(8,128)S(1)} %get-tuple-element.137, f32[32,4,128]{2,1,0:T(4,128)S(1)} %copy.91, f32[32,128]{1,0:T(8,128)S(1)} %get-tuple-element.139, ...), kind=kLoop, calls=%fused_computation.clone.1 | loop fusion | flops 23064576 | bytes 327680 | tf_op jit(solution)/shard_map/while/body/eval_jaxpr/reduce_sum | solution.py:28
  258.4 4.4 %multiply_reduce_fusion.2 = f32[32,128]{1,0:T(8,128)S(1)} fusion(f32[32,4,128]{2,1,0:T(4,128)S(1)} %copy.88, f32[32,128]{1,0:T(8,128)S(1)} %get-tuple-element.135, f32[32,4,128]{2,1,0:T(4,128)S(1)} %copy.90, f32[32,128]{1,0:T(8,128)S(1)} %get-tuple-element.137, f32[32,4,128]{2,1,0:T(4,128)S(1)} %copy.91, f32[32,128]{1,0:T(8,128)S(1)} %get-tuple-element.139, ...), kind=kLoop, calls=%fused_computation.clone.1 | loop fusion | flops 23064576 | bytes 327680 | tf_op jit(solution)/shard_map/while/body/eval_jaxpr/reduce_sum | solution.py:28
  264.9 4.4 %multiply_reduce_fusion.2 = f32[32,128]{1,0:T(8,128)S(1)} fusion(f32[32,4,128]{2,1,0:T(4,128)S(1)} %copy.88, f32[32,128]{1,0:T(8,128)S(1)} %get-tuple-element.135, f32[32,4,128]{2,1,0:T(4,128)S(1)} %copy.90, f32[32,128]{1,0:T(8,128)S(1)} %get-tuple-element.137, f32[32,4,128]{2,1,0:T(4,128)S(1)} %copy.91, f32[32,128]{1,0:T(8,128)S(1)} %get-tuple-element.139, ...), kind=kLoop, calls=%fused_computation.clone.1 | loop fusion | flops 23064576 | bytes 327680 | tf_op jit(solution)/shard_map/while/body/eval_jaxpr/reduce_sum | solution.py:28
  271.4 4.4 %multiply_reduce_fusion.2 = f32[32,128]{1,0:T(8,128)S(1)} fusion(f32[32,4,128]{2,1,0:T(4,128)S(1)} %copy.88, f32[32,128]{1,0:T(8,128)S(1)} %get-tuple-element.135, f32[32,4,128]{2,1,0:T(4,128)S(1)} %copy.90, f32[32,128]{1,0:T(8,128)S(1)} %get-tuple-element.137, f32[32,4,128]{2,1,0:T(4,128)S(1)} %copy.91, f32[32,128]{1,0:T(8,128)S(1)} %get-tuple-element.139, ...), kind=kLoop, calls=%fused_computation.clone.1 | loop fusion | flops 23064576 | bytes 327680 | tf_op jit(solution)/shard_map/while/body/eval_jaxpr/reduce_sum | solution.py:28
  276.5 3.5 all-to-all-start.1
  280.1 1.4 fusion.14
  281.7 75.6 %psum.23 = f32[1024]{0:T(1024)S(1)} all-reduce(f32[1024]{0:T(1024)S(1)} %bitcast.156), channel_id=1, replica_groups=mesh['dom'=16,'grp'=16] {'dom','grp'}, use_global_device_ids=true, to_apply=%region_9.10 | all-reduce | flops 1024 | bytes 8192 | tf_op jit(solution)/shard_map/psum | solution.py:97
  357.9 1.3 convolution_add_fusion
  (240 shorter events, 43.8 us)
Async XLA Ops:
  7.2 157.8 %all-gather.3.cloned.1.call-start = ((), (), s32[]{:S(2)}) async-start(), calls=%async_computation.2 | async-start | bytes 2228224 | tf_op jit(solution)/shard_map/all_gather | solution.py:115
  13.7 23.8 %copy-start.10 = (s32[1,64]{1,0:T(1,128)S(1)}, s32[1,64]{1,0:T(1,128)}, u32[]{:S(2)}) copy-start(s32[1,64]{1,0:T(1,128)} %param.16) | copy-start | bytes 772
  37.1 1.8 copy-start
  37.1 1.8 copy-start.1
  37.1 2.2 copy-start.3
  37.5 3.8 %copy-start.6 = (s32[512,4]{0,1:T(4,128)S(1)}, s32[512,4]{0,1:T(4,128)}, u32[]{:S(2)}) copy-start(s32[512,4]{0,1:T(4,128)} %param.19) | copy-start | bytes 24580
  37.5 4.5 %copy-start.11 = (s32[1,16]{1,0:T(1,128)S(1)}, s32[1,16]{1,0:T(1,128)}, u32[]{:S(2)}) copy-start(s32[1,16]{1,0:T(1,128)} %param.18) | copy-start | bytes 196
  37.5 19.0 %copy-start.7 = (s32[1,16,16]{2,1,0:T(8,128)S(1)}, s32[1,16,16]{2,1,0:T(8,128)}, u32[]{:S(2)}) copy-start(s32[1,16,16]{2,1,0:T(8,128)} %param.17) | copy-start | bytes 3076
  39.3 125.7 %copy-start.12 = (s32[16]{0:T(128)}, s32[16]{0:T(128)S(1)}, u32[]{:S(2)}) copy-start(s32[16]{0:T(128)S(1)} %and_select_fusion) | copy-start | bytes 196
  39.4 125.6 %copy-start.4 = (s32[32768]{0:T(1024)}, s32[32768]{0:T(1024)S(1)}, u32[]{:S(2)}) copy-start(s32[32768]{0:T(1024)S(1)} %add_select_fusion) | copy-start | bytes 393220
  162.8 1.4 copy-start.8
  171.8 108.3 %copy-start.2 = (f32[32768]{0:T(1024)S(1)}, f32[32768]{0:T(1024)}, u32[]{:S(2)}) copy-start(f32[32768]{0:T(1024)} %multiply_multiply_fusion) | copy-start | bytes 393220
  171.8 108.3 %copy-start.5 = (s32[32768]{0:T(1024)S(1)}, s32[32768]{0:T(1024)}, u32[]{:S(2)}) copy-start(s32[32768]{0:T(1024)} %copy-done.4) | copy-start | bytes 393220
  171.8 109.7 %copy-start.13 = (s32[16]{0:T(128)S(1)}, s32[16]{0:T(128)}, u32[]{:S(2)}) copy-start(s32[16]{0:T(128)} %copy-done.12) | copy-start | bytes 196
  171.8 185.5 %copy-start.9 = (f32[1024]{0:T(1024)S(1)}, f32[1024]{0:T(1024)}, u32[]{:S(2)}) copy-start(f32[1024]{0:T(1024)} %copy-done.8) | copy-start | bytes 12292
  276.5 81.4 %all-to-all-start.1 = ((f32[16,32,128]{2,1,0:T(8,128)}), f32[16,32,128]{2,1,0:T(8,128)S(1)}, u32[]{:S(2)}, u32[]{:S(2)}) async-start(f32[16,32,128]{2,1,0:T(8,128)} %broadcast_multiply_fusion), calls=%async_computation.1 | async-start | bytes 524288 | tf_op jit(solution)/shard_map/all_to_all | solution.py:131
Sparse Core Ops, SparseCore 0:
  39.0 48.9 all-gather.2
where the time goes:
time: 367 us; the launch traced here: 366 us
  blocking collectives  219 us (60%)
  other arithmetic  77.5 us (21%)
  matrix products  26 us (7%)
  local copies, waits for them, and re-layouts  23.5 us (6%)
  between operations  14.4 us (4%)
    psum x1, blocking collectives, shards(): lax.psum((first_sums[0], first_sums[1:]), ('dom', 'grp'))  89 us
    psum x1, blocking collectives, shards(): lax.psum(group_sums((mass_flat * kinetic)[None, :])[0], ('dom', 'grp'))  75.6 us
    reduce_sum x16, other arithmetic, tile_potential(): return -jnp.sum(weights, axis=(1, 3))  70.1 us
    all_to_all x1, blocking collectives, shards(): lax.all_to_all(outgoing, 'grp', split_axis=0, concat_axis=0, tiled=True)  23.4 us
    dot_general x18, matrix products, select_rows(): jnp.dot(picker, flat, precision=exact, preferred_element_type=jnp.float32)  19.3 us
    all_gather x1, blocking collectives, shards(): lax.all_gather(send_list, 'grp', axis=0, tiled=True)  17.3 us
    all_gather x1, blocking collectives, shards(): lax.all_gather(send_count, 'grp', axis=0, tiled=True)  14.1 us
    dynamic_slice x48, local copies, waits for them, and re-layouts, slot_potential(): lax.map(one_block, (owned.reshape(slot_count // block_rows, block_rows, 4...  12.1 us
  transfers between devices with their start and end apart: 2, of which 0 were waited for; matrix products, arithmetic and copies ran while one was open for 2% of the time, Pallas kernels for 0%

commit v1 on v0

--- a/solution.py
+++ b/solution.py
@@ -94,7 +94,8 @@
     per_particle = jnp.dot(bulk_local, member, precision=exact, preferred_element_type=jnp.float32)
     relative = speeds - per_particle
     kinetic = 0.5 * jnp.sum(relative * relative, axis=0)
-    heat_sum = lax.psum(group_sums((mass_flat * kinetic)[None, :])[0], ("dom", "grp"))
+    v0 = group_sums((mass_flat * kinetic)[None, :])[0]
+    heat_sum = jax.lax.all_gather(v0, ("dom", "grp")).sum(axis=0)
     group_kinetic = heat_sum / mass_total
     onehot = (destination[:, None] == jnp.arange(owners, dtype=jnp.int32)[None, :]).astype(
         jnp.int32

time: 367 us -> 299 us (0.81)
  the two profiles are of different devices: /device:TPU:1 before, /device:TPU:2 now
where the time goes in v1:
time: 299 us; the launch traced here: 297 us
  blocking collectives  142 us (47%)
  other arithmetic  77 us (26%)
  matrix products  26.6 us (9%)
  local copies, waits for them, and re-layouts  24.8 us (8%)
  between operations  14.3 us (5%)
  starting transfers between devices  6.03 us (2%)
  waiting for transfers between devices  5.28 us (2%)
    psum x1, blocking collectives, shards(): lax.psum((first_sums[0], first_sums[1:]), ('dom', 'grp'))  77 us
    reduce_sum x16, other arithmetic, tile_potential(): return -jnp.sum(weights, axis=(1, 3))  70.1 us
    all_to_all x1, blocking collectives, shards(): lax.all_to_all(outgoing, 'grp', split_axis=0, concat_axis=0, tiled=True)  23.1 us
    all_gather x1, blocking collectives, shards(): lax.all_gather(send_list, 'grp', axis=0, tiled=True)  21.5 us
    all_gather x1, blocking collectives, shards(): lax.all_gather(send_count, 'grp', axis=0, tiled=True)  20.2 us
    dot_general x18, matrix products, select_rows(): jnp.dot(picker, flat, precision=exact, preferred_element_type=jnp.float32)  19.3 us
    dynamic_slice x48, local copies, waits for them, and re-layouts, slot_potential(): lax.map(one_block, (owned.reshape(slot_count // block_rows, block_rows, 4...  12 us
  transfers between devices with their start and end apart: 3, of which 1 were waited for; matrix products, arithmetic and copies ran while one was open for 40% of the time, Pallas kernels for 0%

profile of v1, /device:TPU:2, one launch (start us, length us, event | category | flops | bytes accessed | tf_op | source)
XLA Modules:
  0.0 297.4 jit_solution(3373814806902413359)
XLA Ops:
  13.7 23.1 %all_to_all.14 = f32[512,4,128]{2,1,0:T(4,128)S(1)} all-to-all(f32[512,4,128]{2,1,0:T(4,128)S(1)} %copy.64), channel_id=1, replica_groups=mesh['dom'=16,'grp'=16] {'grp'}, dimensions={0} | all-to-all | bytes 2097152 | tf_op jit(solution)/shard_map/all_to_all | solution.py:112
  37.1 1.4 fusion.15
  39.0 1.6 fusion.9
  40.9 77.0 %all-reduce = (f32[3,1024]{1,0:T(4,128)S(1)}, f32[1024]{0:T(1024)S(1)}) all-reduce(f32[3,1024]{1,0:T(4,128)S(1)} %slice.60, f32[1024]{0:T(1024)S(1)} %bitcast.154), channel_id=1, replica_groups=mesh['dom'=16,'grp'=16] {'dom','grp'}, use_global_device_ids=true, to_apply=%region_0.1 | all-reduce | flops 4096 | bytes 32768 | tf_op jit(solution)/shard_map/psum | solution.py:89
  119.3 1.4 fusion.14
  121.6 21.5 %all_gather.13 = s32[16,16,16]{2,1,0:T(8,128)S(1)} all-gather(s32[1,16,16]{2,1,0:T(8,128)S(1)} %copy-done.3), channel_id=1, replica_groups=mesh['dom'=16,'grp'=16] {'grp'}, dimensions={0}, use_global_device_ids=true | all-gather | bytes 17408 | tf_op jit(solution)/shard_map/all_gather | solution.py:118
  143.1 20.2 %all-gather.1 = s32[16,1,16]{2,1,0:T(1,128)S(1)} all-gather(s32[1,1,16]{2,1,0:T(1,128)S(1)} %bitcast.158), channel_id=1, replica_groups=mesh['dom'=16,'grp'=16] {'grp'}, dimensions={0}, use_global_device_ids=true | all-gather | bytes 1088 | tf_op jit(solution)/shard_map/all_gather | solution.py:119
  164.6 1.9 copy.66
  166.5 1.3 fusion.10
  168.2 1.5 pad_maximum_fusion
  169.7 1.7 copy.70
  171.4 103.9 %while.12 = (s32[]{:T(128)}, f32[16,32,128]{2,1,0:T(8,128)S(1)}, s32[16,32,4]{1,0,2:T(8,128)}, f32[768,4,128]{0,2,1:T(8,128)S(1)}, f32[16,32,4,128]{3,2,1,0:T(4,128)S(1)}, /*index=5*/s32[]{:T(128)}) while((s32[]{:T(128)}, f32[16,32,128]{2,1,0:T(8,128)S(1)}, s32[16,32,4]{1,0,2:T(8,128)}, f32[768,4,128]{0,2,1:T(8,128)S(1)}, ...), condition=%wide.region_8.9_spmd, body=%wide.region_6.8_spmd.sunk | while | flops 627146752 | bytes 3606097 | solution.py:41
  173.5 4.4 %multiply_reduce_fusion.2 = f32[32,128]{1,0:T(8,128)S(1)} fusion(f32[32,4,128]{2,1,0:T(4,128)S(1)} %copy.88, f32[32,128]{1,0:T(8,128)S(1)} %get-tuple-element.135, f32[32,4,128]{2,1,0:T(4,128)S(1)} %copy.90, f32[32,128]{1,0:T(8,128)S(1)} %get-tuple-element.137, f32[32,4,128]{2,1,0:T(4,128)S(1)} %copy.91, f32[32,128]{1,0:T(8,128)S(1)} %get-tuple-element.139, ...), kind=kLoop, calls=%fused_computation.clone.1 | loop fusion | flops 23064576 | bytes 327680 | tf_op jit(solution)/shard_map/while/body/eval_jaxpr/reduce_sum | solution.py:28
  180.0 4.4 %multiply_reduce_fusion.2 = f32[32,128]{1,0:T(8,128)S(1)} fusion(f32[32,4,128]{2,1,0:T(4,128)S(1)} %copy.88, f32[32,128]{1,0:T(8,128)S(1)} %get-tuple-element.135, f32[32,4,128]{2,1,0:T(4,128)S(1)} %copy.90, f32[32,128]{1,0:T(8,128)S(1)} %get-tuple-element.137, f32[32,4,128]{2,1,0:T(4,128)S(1)} %copy.91, f32[32,128]{1,0:T(8,128)S(1)} %get-tuple-element.139, ...), kind=kLoop, calls=%fused_computation.clone.1 | loop fusion | flops 23064576 | bytes 327680 | tf_op jit(solution)/shard_map/while/body/eval_jaxpr/reduce_sum | solution.py:28
  186.5 4.4 %multiply_reduce_fusion.2 = f32[32,128]{1,0:T(8,128)S(1)} fusion(f32[32,4,128]{2,1,0:T(4,128)S(1)} %copy.88, f32[32,128]{1,0:T(8,128)S(1)} %get-tuple-element.135, f32[32,4,128]{2,1,0:T(4,128)S(1)} %copy.90, f32[32,128]{1,0:T(8,128)S(1)} %get-tuple-element.137, f32[32,4,128]{2,1,0:T(4,128)S(1)} %copy.91, f32[32,128]{1,0:T(8,128)S(1)} %get-tuple-element.139, ...), kind=kLoop, calls=%fused_computation.clone.1 | loop fusion | flops 23064576 | bytes 327680 | tf_op jit(solution)/shard_map/while/body/eval_jaxpr/reduce_sum | solution.py:28
  193.0 4.4 %multiply_reduce_fusion.2 = f32[32,128]{1,0:T(8,128)S(1)} fusion(f32[32,4,128]{2,1,0:T(4,128)S(1)} %copy.88, f32[32,128]{1,0:T(8,128)S(1)} %get-tuple-element.135, f32[32,4,128]{2,1,0:T(4,128)S(1)} %copy.90, f32[32,128]{1,0:T(8,128)S(1)} %get-tuple-element.137, f32[32,4,128]{2,1,0:T(4,128)S(1)} %copy.91, f32[32,128]{1,0:T(8,128)S(1)} %get-tuple-element.139, ...), kind=kLoop, calls=%fused_computation.clone.1 | loop fusion | flops 23064576 | bytes 327680 | tf_op jit(solution)/shard_map/while/body/eval_jaxpr/reduce_sum | solution.py:28
  199.4 4.4 %multiply_reduce_fusion.2 = f32[32,128]{1,0:T(8,128)S(1)} fusion(f32[32,4,128]{2,1,0:T(4,128)S(1)} %copy.88, f32[32,128]{1,0:T(8,128)S(1)} %get-tuple-element.135, f32[32,4,128]{2,1,0:T(4,128)S(1)} %copy.90, f32[32,128]{1,0:T(8,128)S(1)} %get-tuple-element.137, f32[32,4,128]{2,1,0:T(4,128)S(1)} %copy.91, f32[32,128]{1,0:T(8,128)S(1)} %get-tuple-element.139, ...), kind=kLoop, calls=%fused_computation.clone.1 | loop fusion | flops 23064576 | bytes 327680 | tf_op jit(solution)/shard_map/while/body/eval_jaxpr/reduce_sum | solution.py:28
  205.9 4.4 %multiply_reduce_fusion.2 = f32[32,128]{1,0:T(8,128)S(1)} fusion(f32[32,4,128]{2,1,0:T(4,128)S(1)} %copy.88, f32[32,128]{1,0:T(8,128)S(1)} %get-tuple-element.135, f32[32,4,128]{2,1,0:T(4,128)S(1)} %copy.90, f32[32,128]{1,0:T(8,128)S(1)} %get-tuple-element.137, f32[32,4,128]{2,1,0:T(4,128)S(1)} %copy.91, f32[32,128]{1,0:T(8,128)S(1)} %get-tuple-element.139, ...), kind=kLoop, calls=%fused_computation.clone.1 | loop fusion | flops 23064576 | bytes 327680 | tf_op jit(solution)/shard_map/while/body/eval_jaxpr/reduce_sum | solution.py:28
  212.4 4.4 %multiply_reduce_fusion.2 = f32[32,128]{1,0:T(8,128)S(1)} fusion(f32[32,4,128]{2,1,0:T(4,128)S(1)} %copy.88, f32[32,128]{1,0:T(8,128)S(1)} %get-tuple-element.135, f32[32,4,128]{2,1,0:T(4,128)S(1)} %copy.90, f32[32,128]{1,0:T(8,128)S(1)} %get-tuple-element.137, f32[32,4,128]{2,1,0:T(4,128)S(1)} %copy.91, f32[32,128]{1,0:T(8,128)S(1)} %get-tuple-element.139, ...), kind=kLoop, calls=%fused_computation.clone.1 | loop fusion | flops 23064576 | bytes 327680 | tf_op jit(solution)/shard_map/while/body/eval_jaxpr/reduce_sum | solution.py:28
  218.9 4.4 %multiply_reduce_fusion.2 = f32[32,128]{1,0:T(8,128)S(1)} fusion(f32[32,4,128]{2,1,0:T(4,128)S(1)} %copy.88, f32[32,128]{1,0:T(8,128)S(1)} %get-tuple-element.135, f32[32,4,128]{2,1,0:T(4,128)S(1)} %copy.90, f32[32,128]{1,0:T(8,128)S(1)} %get-tuple-element.137, f32[32,4,128]{2,1,0:T(4,128)S(1)} %copy.91, f32[32,128]{1,0:T(8,128)S(1)} %get-tuple-element.139, ...), kind=kLoop, calls=%fused_computation.clone.1 | loop fusion | flops 23064576 | bytes 327680 | tf_op jit(solution)/shard_map/while/body/eval_jaxpr/reduce_sum | solution.py:28
  225.4 4.4 %multiply_reduce_fusion.2 = f32[32,128]{1,0:T(8,128)S(1)} fusion(f32[32,4,128]{2,1,0:T(4,128)S(1)} %copy.88, f32[32,128]{1,0:T(8,128)S(1)} %get-tuple-element.135, f32[32,4,128]{2,1,0:T(4,128)S(1)} %copy.90, f32[32,128]{1,0:T(8,128)S(1)} %get-tuple-element.137, f32[32,4,128]{2,1,0:T(4,128)S(1)} %copy.91, f32[32,128]{1,0:T(8,128)S(1)} %get-tuple-element.139, ...), kind=kLoop, calls=%fused_computation.clone.1 | loop fusion | flops 23064576 | bytes 327680 | tf_op jit(solution)/shard_map/while/body/eval_jaxpr/reduce_sum | solution.py:28
  231.9 4.4 %multiply_reduce_fusion.2 = f32[32,128]{1,0:T(8,128)S(1)} fusion(f32[32,4,128]{2,1,0:T(4,128)S(1)} %copy.88, f32[32,128]{1,0:T(8,128)S(1)} %get-tuple-element.135, f32[32,4,128]{2,1,0:T(4,128)S(1)} %copy.90, f32[32,128]{1,0:T(8,128)S(1)} %get-tuple-element.137, f32[32,4,128]{2,1,0:T(4,128)S(1)} %copy.91, f32[32,128]{1,0:T(8,128)S(1)} %get-tuple-element.139, ...), kind=kLoop, calls=%fused_computation.clone.1 | loop fusion | flops 23064576 | bytes 327680 | tf_op jit(solution)/shard_map/while/body/eval_jaxpr/reduce_sum | solution.py:28
  238.4 4.4 %multiply_reduce_fusion.2 = f32[32,128]{1,0:T(8,128)S(1)} fusion(f32[32,4,128]{2,1,0:T(4,128)S(1)} %copy.88, f32[32,128]{1,0:T(8,128)S(1)} %get-tuple-element.135, f32[32,4,128]{2,1,0:T(4,128)S(1)} %copy.90, f32[32,128]{1,0:T(8,128)S(1)} %get-tuple-element.137, f32[32,4,128]{2,1,0:T(4,128)S(1)} %copy.91, f32[32,128]{1,0:T(8,128)S(1)} %get-tuple-element.139, ...), kind=kLoop, calls=%fused_computation.clone.1 | loop fusion | flops 23064576 | bytes 327680 | tf_op jit(solution)/shard_map/while/body/eval_jaxpr/reduce_sum | solution.py:28
  244.9 4.4 %multiply_reduce_fusion.2 = f32[32,128]{1,0:T(8,128)S(1)} fusion(f32[32,4,128]{2,1,0:T(4,128)S(1)} %copy.88, f32[32,128]{1,0:T(8,128)S(1)} %get-tuple-element.135, f32[32,4,128]{2,1,0:T(4,128)S(1)} %copy.90, f32[32,128]{1,0:T(8,128)S(1)} %get-tuple-element.137, f32[32,4,128]{2,1,0:T(4,128)S(1)} %copy.91, f32[32,128]{1,0:T(8,128)S(1)} %get-tuple-element.139, ...), kind=kLoop, calls=%fused_computation.clone.1 | loop fusion | flops 23064576 | bytes 327680 | tf_op jit(solution)/shard_map/while/body/eval_jaxpr/reduce_sum | solution.py:28
  251.4 4.4 %multiply_reduce_fusion.2 = f32[32,128]{1,0:T(8,128)S(1)} fusion(f32[32,4,128]{2,1,0:T(4,128)S(1)} %copy.88, f32[32,128]{1,0:T(8,128)S(1)} %get-tuple-element.135, f32[32,4,128]{2,1,0:T(4,128)S(1)} %copy.90, f32[32,128]{1,0:T(8,128)S(1)} %get-tuple-element.137, f32[32,4,128]{2,1,0:T(4,128)S(1)} %copy.91, f32[32,128]{1,0:T(8,128)S(1)} %get-tuple-element.139, ...), kind=kLoop, calls=%fused_computation.clone.1 | loop fusion | flops 23064576 | bytes 327680 | tf_op jit(solution)/shard_map/while/body/eval_jaxpr/reduce_sum | solution.py:28
  257.9 4.4 %multiply_reduce_fusion.2 = f32[32,128]{1,0:T(8,128)S(1)} fusion(f32[32,4,128]{2,1,0:T(4,128)S(1)} %copy.88, f32[32,128]{1,0:T(8,128)S(1)} %get-tuple-element.135, f32[32,4,128]{2,1,0:T(4,128)S(1)} %copy.90, f32[32,128]{1,0:T(8,128)S(1)} %get-tuple-element.137, f32[32,4,128]{2,1,0:T(4,128)S(1)} %copy.91, f32[32,128]{1,0:T(8,128)S(1)} %get-tuple-element.139, ...), kind=kLoop, calls=%fused_computation.clone.1 | loop fusion | flops 23064576 | bytes 327680 | tf_op jit(solution)/shard_map/while/body/eval_jaxpr/reduce_sum | solution.py:28
  264.4 4.4 %multiply_reduce_fusion.2 = f32[32,128]{1,0:T(8,128)S(1)} fusion(f32[32,4,128]{2,1,0:T(4,128)S(1)} %copy.88, f32[32,128]{1,0:T(8,128)S(1)} %get-tuple-element.135, f32[32,4,128]{2,1,0:T(4,128)S(1)} %copy.90, f32[32,128]{1,0:T(8,128)S(1)} %get-tuple-element.137, f32[32,4,128]{2,1,0:T(4,128)S(1)} %copy.91, f32[32,128]{1,0:T(8,128)S(1)} %get-tuple-element.139, ...), kind=kLoop, calls=%fused_computation.clone.1 | loop fusion | flops 23064576 | bytes 327680 | tf_op jit(solution)/shard_map/while/body/eval_jaxpr/reduce_sum | solution.py:28
  270.9 4.4 %multiply_reduce_fusion.2 = f32[32,128]{1,0:T(8,128)S(1)} fusion(f32[32,4,128]{2,1,0:T(4,128)S(1)} %copy.88, f32[32,128]{1,0:T(8,128)S(1)} %get-tuple-element.135, f32[32,4,128]{2,1,0:T(4,128)S(1)} %copy.90, f32[32,128]{1,0:T(8,128)S(1)} %get-tuple-element.137, f32[32,4,128]{2,1,0:T(4,128)S(1)} %copy.91, f32[32,128]{1,0:T(8,128)S(1)} %get-tuple-element.139, ...), kind=kLoop, calls=%fused_computation.clone.1 | loop fusion | flops 23064576 | bytes 327680 | tf_op jit(solution)/shard_map/while/body/eval_jaxpr/reduce_sum | solution.py:28
  276.0 6.0 %all-to-all-start.1 = ((f32[16,32,128]{2,1,0:T(8,128)}), f32[16,32,128]{2,1,0:T(8,128)S(1)}, u32[]{:S(2)}, u32[]{:S(2)}) async-start(f32[16,32,128]{2,1,0:T(8,128)} %broadcast_multiply_fusion), calls=%async_computation.1 | async-start | bytes 524288 | tf_op jit(solution)/shard_map/all_to_all | solution.py:132
  282.0 1.4 reshape.284
  284.1 5.2 %all-to-all-done.1 = f32[16,32,128]{2,1,0:T(8,128)S(1)} async-done(((f32[16,32,128]{2,1,0:T(8,128)}), f32[16,32,128]{2,1,0:T(8,128)S(1)}, u32[]{:S(2)}, u32[]{:S(2)}) %all-to-all-start.1) | async-done | bytes 262176 | tf_op jit(solution)/shard_map/all_to_all | solution.py:132
  289.3 1.3 convolution_add_fusion
  (234 shorter events, 45.0 us)
Async XLA Ops:
  7.2 157.5 %all-gather.5.cloned.1.call-start = ((), (), s32[]{:S(2)}) async-start(), calls=%async_computation.2 | async-start | bytes 2228224 | tf_op jit(solution)/shard_map/all_gather | solution.py:116
  13.7 23.5 %copy-start.7 = (s32[1,64]{1,0:T(1,128)S(1)}, s32[1,64]{1,0:T(1,128)}, u32[]{:S(2)}) copy-start(s32[1,64]{1,0:T(1,128)} %param.16) | copy-start | bytes 772
  36.7 1.8 copy-start
  36.7 1.8 copy-start.1
  36.7 2.2 copy-start.2
  38.5 243.5 %all-gather.7.cloned.1.call-start = ((), (), s32[]{:S(2)}) async-start(), calls=%async_computation.3 | async-start | bytes 1052672 | tf_op jit(solution)/shard_map/all_gather | solution.py:98
  39.0 82.6 %copy-start.3 = (s32[1,16,16]{2,1,0:T(8,128)S(1)}, s32[1,16,16]{2,1,0:T(8,128)}, u32[]{:S(2)}) copy-start(s32[1,16,16]{2,1,0:T(8,128)} %param.17) | copy-start | bytes 3076
  39.0 104.1 %copy-start.8 = (s32[1,16]{1,0:T(1,128)S(1)}, s32[1,16]{1,0:T(1,128)}, u32[]{:S(2)}) copy-start(s32[1,16]{1,0:T(1,128)} %param.18) | copy-start | bytes 196
  39.0 124.8 %copy-start.4 = (s32[512,4]{0,1:T(4,128)S(1)}, s32[512,4]{0,1:T(4,128)}, u32[]{:S(2)}) copy-start(s32[512,4]{0,1:T(4,128)} %param.19) | copy-start | bytes 24580
  118.0 46.6 %copy-start.5 = (f32[1024]{0:T(1024)}, f32[1024]{0:T(1024)S(1)}, u32[]{:S(2)}) copy-start(f32[1024]{0:T(1024)S(1)} %get-tuple-element.88) | copy-start | bytes 12292
  275.3 8.2 %copy-start.6 = (f32[1024]{0:T(1024)S(1)}, f32[1024]{0:T(1024)}, u32[]{:S(2)}) copy-start(f32[1024]{0:T(1024)} %copy-done.5) | copy-start | bytes 12292
  276.0 13.3 %all-to-all-start.1 = ((f32[16,32,128]{2,1,0:T(8,128)}), f32[16,32,128]{2,1,0:T(8,128)S(1)}, u32[]{:S(2)}, u32[]{:S(2)}) async-start(f32[16,32,128]{2,1,0:T(8,128)} %broadcast_multiply_fusion), calls=%async_computation.1 | async-start | bytes 524288 | tf_op jit(solution)/shard_map/all_to_all | solution.py:132
Sparse Core Ops, SparseCore 0:
  38.6 49.7 all-gather.4
  121.7 99.1 all-gather.6
